TPU v7x, 512 devices: a whole 4x8x8 slice. The times are simulated.
512 devices in a mesh: grp: 16 (over y, core), dev: 32 (over z, x).
Axes of the slice: x: 4, y: 8, z: 8, core: 2. Of those that a mesh axis runs over, the one named last changes fastest.
Arguments:
- panel_inverse: float32 [16, 32, 256, 256], P('grp', 'dev')
- coupling: float32 [16, 32, 256, 256], P('grp', 'dev'), may hold values from -0.875 to 0.875
- loads: float32 [16, 32, 16, 256], P('grp', 'dev'), may hold values from -6 to 6
- stiffness: float32 [24, 24], replicated
- element_substructure: int32 [16, 32, 1024], P('grp', 'dev'), may hold values from 0 to 31
- element_rows: int32 [16, 32, 24, 1024], P('grp', 'dev'), may hold values from 0 to 255
- element_density: float32 [16, 32, 1024], P('grp', 'dev'), may hold values from 0.2 to 1
- send_elements: int32 [16, 32, 32, 64], P('grp', 'dev'), may hold values from 0 to 1023
- receive_cells: int32 [16, 32, 32, 64], P('grp', 'dev'), may hold values from -1 to 16383, as said below
- design_density: float32 [16, 32, 128, 128], P('grp', 'dev'), may hold values from 0.3 to 1
- filter_offsets: int32 [8], replicated, may hold values from -3 to 3, as said below
- filter_weights: float32 [8], replicated, may hold values from 0.2 to 1
Outputs:
- interface: float32 [16, 32, 16, 256], P('grp', 'dev')
- filtered: float32 [16, 32, 128, 128], P('grp', 'dev')
Inputs may be any that keep to these rules, and one draw needn't show every extreme that they name: `receive_cells`: each receiver's slots from one source are filled in order: the first 64, 32, 16 or 8 hold a cell, the rest -1; in every group one owner is full from every source. `filter_offsets`: the offsets -3 and 3 are always among them; offsets may repeat.
All inputs are finite; a program needn't handle non-finite values.
Results may differ from a plain program's by a relative error of at most 0.0003.
Values sent between devices are 32-bit elements; how exact they have to be, the bound alone decides.
No kernel may reach another device: no remote copies, remote signals or barrier semaphores. Data moves between devices by JAX's collectives and lax.ppermute only.
A program may use at most 64 MiB of HBM per device.

v0:
```python
import jax
import jax.numpy as jnp
from jax import lax
from jax.sharding import PartitionSpec as P

NK = 8
RADIUS = 3
exact_mode = lax.Precision.HIGHEST
penalty = 3.0
energy_scale = 1.0 / 4096.0


def passed_along(value, axis, steps):
    count = lax.axis_size(axis)
    leading, last = (max(0, -steps), min(count, count - steps))
    return lax.ppermute(value, axis, [(source, source + steps) for source in range(leading, last)])


def padded_2(cells, sides, width):
    for axis, dim in sides:
        count = lax.axis_size(axis)
        ends = count - 1
        head = lax.slice_in_dim(cells, 0, width, axis=dim)
        tail = lax.slice_in_dim(cells, cells.shape[dim] - width, cells.shape[dim], axis=dim)
        cells = jnp.concatenate(
            [
                lax.ppermute(tail, axis, [(i, (i + 1) % count) for i in range(ends)]),
                cells,
                lax.ppermute(head, axis, [((i + 1) % count, i) for i in range(ends)]),
            ],
            axis=dim,
        )
    return cells


def product(left, right):
    return jnp.dot(left, right, precision=exact_mode, preferred_element_type=jnp.float32)


def on_device(
    panel_inverse,
    coupling,
    loads,
    stiffness,
    element_substructure,
    element_rows,
    element_density,
    send_elements,
    receive_cells,
    design_density,
    filter_offsets,
    filter_weights,
):
    inverse = panel_inverse[0, 0]
    couple = coupling[0, 0]
    rights = loads[0, 0]
    source = product(rights, inverse)

    def advance(level, current):
        previous = passed_along(current, "grp", 1)
        return product(rights - product(previous, couple), inverse)

    solved = lax.fori_loop(0, lax.axis_size("grp") - 1, advance, source)
    columns = lax.all_gather(solved, "dev", axis=1, tiled=True)
    panel_order = solved.shape[1]
    lookup = element_substructure[0, 0][None, :] * panel_order + element_rows[0, 0]
    motion = jnp.take(columns, lookup, axis=1)
    forces = jnp.einsum("ij,lje->lie", stiffness, motion, precision=exact_mode)
    energy = jnp.sum(motion * forces, axis=(0, 1))
    density = element_density[0, 0]
    sensitivity = -penalty * density * density * energy * energy_scale
    outgoing = jnp.take(sensitivity, send_elements[0, 0], axis=0)
    received = lax.all_to_all(outgoing, "dev", split_axis=0, concat_axis=0, tiled=True)
    owned = design_density[0, 0]
    row_count = owned.shape[0]
    cells = row_count * 128
    targets = receive_cells[0, 0]
    segment_ids = jnp.where(targets >= 0, targets, cells)
    collected = jax.ops.segment_sum(received.ravel(), segment_ids.ravel(), num_segments=cells + 1)[
        :cells
    ]
    weighted = owned * collected.reshape(row_count, 128)
    padded = padded_2(weighted, (("dev", 0),), RADIUS)
    total_rows = lax.axis_size("dev") * row_count
    global_rows = lax.axis_index("dev") * row_count + jnp.arange(row_count, dtype=jnp.int32)
    accum = jnp.zeros((row_count, 128), jnp.float32)
    weight_sum = jnp.zeros((row_count,), jnp.float32)
    for which in range(NK):
        offset = filter_offsets[which]
        window_rows = lax.dynamic_slice_in_dim(padded, RADIUS + offset, row_count, 0)
        inside = ((global_rows + offset >= 0) & (global_rows + offset < total_rows)).astype(
            jnp.float32
        )
        accum = accum + filter_weights[which] * window_rows
        weight_sum = weight_sum + filter_weights[which] * inside
    filtered = accum / (owned * weight_sum[:, None])
    return (solved[None, None], filtered[None, None])


def solution(mesh):
    placed = (
        P("grp", "dev", None, None),
        P("grp", "dev", None, None),
        P("grp", "dev", None, None),
        P(),
        P("grp", "dev", None),
        P("grp", "dev", None, None),
        P("grp", "dev", None),
        P("grp", "dev", None, None),
        P("grp", "dev", None, None),
        P("grp", "dev", None, None),
        P(),
        P(),
    )
    return jax.shard_map(
        on_device,
        mesh=mesh,
        in_specs=placed,
        out_specs=(P("grp", "dev", None, None), P("grp", "dev", None, None)),
        check_vma=False,
    )
```

profile of v0, /device:TPU:38, one launch (start us, length us, event | category | flops | bytes accessed | tf_op | source)
XLA Modules:
  0.0 357.8 jit_solution(10545197386665113381)
XLA Ops:
  4.4 129.7 %while.10 = (s32[]{:T(128)}, f32[16,256]{1,0:T(8,128)S(1)}, f32[256,256]{1,0:T(8,128)}, f32[16,256]{1,0:T(8,128)}, f32[256,256]{1,0:T(8,128)}, /*index=5*/s32[]{:T(128)}) while((s32[]{:T(128)}, f32[16,256]{1,0:T(8,128)S(1)}, f32[256,256]{1,0:T(8,128)}, f32[16,256]{1,0:T(8,128)}, f32[256,256]{1,0:T(8,128)}, /*index=5*/s32[]{:T(128)}) %tuple.42), condition=%wide.region_1.0_spmd, body=%wide.region_0.0_spmd.sunk | while | flops 25169920 | bytes 671853 | solution.py:63
  4.4 1.9 collective-permute-start
  6.3 4.3 %collective-permute-done = f32[16,256]{1,0:T(8,128)S(1)} collective-permute-done((f32[16,256]{1,0:T(8,128)S(1)}, f32[16,256]{1,0:T(8,128)S(1)}, u32[]{:S(2)}, u32[]{:S(2)}) %collective-permute-start) | collective-permute-done | bytes 16416 | tf_op jit(solution)/shard_map/while/body/eval_jaxpr/ppermute | solution.py:16
  10.7 1.2 convolution_subtract_fusion.2
  13.0 1.9 collective-permute-start
  15.0 4.3 %collective-permute-done = f32[16,256]{1,0:T(8,128)S(1)} collective-permute-done((f32[16,256]{1,0:T(8,128)S(1)}, f32[16,256]{1,0:T(8,128)S(1)}, u32[]{:S(2)}, u32[]{:S(2)}) %collective-permute-start) | collective-permute-done | bytes 16416 | tf_op jit(solution)/shard_map/while/body/eval_jaxpr/ppermute | solution.py:16
  19.3 1.2 convolution_subtract_fusion.2
  21.7 1.9 collective-permute-start
  23.6 4.3 %collective-permute-done = f32[16,256]{1,0:T(8,128)S(1)} collective-permute-done((f32[16,256]{1,0:T(8,128)S(1)}, f32[16,256]{1,0:T(8,128)S(1)}, u32[]{:S(2)}, u32[]{:S(2)}) %collective-permute-start) | collective-permute-done | bytes 16416 | tf_op jit(solution)/shard_map/while/body/eval_jaxpr/ppermute | solution.py:16
  27.9 1.2 convolution_subtract_fusion.2
  30.3 1.9 collective-permute-start
  32.3 4.3 %collective-permute-done = f32[16,256]{1,0:T(8,128)S(1)} collective-permute-done((f32[16,256]{1,0:T(8,128)S(1)}, f32[16,256]{1,0:T(8,128)S(1)}, u32[]{:S(2)}, u32[]{:S(2)}) %collective-permute-start) | collective-permute-done | bytes 16416 | tf_op jit(solution)/shard_map/while/body/eval_jaxpr/ppermute | solution.py:16
  36.6 1.2 convolution_subtract_fusion.2
  39.0 1.9 collective-permute-start
  40.9 4.3 %collective-permute-done = f32[16,256]{1,0:T(8,128)S(1)} collective-permute-done((f32[16,256]{1,0:T(8,128)S(1)}, f32[16,256]{1,0:T(8,128)S(1)}, u32[]{:S(2)}, u32[]{:S(2)}) %collective-permute-start) | collective-permute-done | bytes 16416 | tf_op jit(solution)/shard_map/while/body/eval_jaxpr/ppermute | solution.py:16
  45.2 1.2 convolution_subtract_fusion.2
  47.6 1.9 collective-permute-start
  49.5 4.3 %collective-permute-done = f32[16,256]{1,0:T(8,128)S(1)} collective-permute-done((f32[16,256]{1,0:T(8,128)S(1)}, f32[16,256]{1,0:T(8,128)S(1)}, u32[]{:S(2)}, u32[]{:S(2)}) %collective-permute-start) | collective-permute-done | bytes 16416 | tf_op jit(solution)/shard_map/while/body/eval_jaxpr/ppermute | solution.py:16
  53.9 1.2 convolution_subtract_fusion.2
  56.3 1.9 collective-permute-start
  58.2 4.3 %collective-permute-done = f32[16,256]{1,0:T(8,128)S(1)} collective-permute-done((f32[16,256]{1,0:T(8,128)S(1)}, f32[16,256]{1,0:T(8,128)S(1)}, u32[]{:S(2)}, u32[]{:S(2)}) %collective-permute-start) | collective-permute-done | bytes 16416 | tf_op jit(solution)/shard_map/while/body/eval_jaxpr/ppermute | solution.py:16
  64.9 1.9 collective-permute-start
  66.8 4.3 %collective-permute-done = f32[16,256]{1,0:T(8,128)S(1)} collective-permute-done((f32[16,256]{1,0:T(8,128)S(1)}, f32[16,256]{1,0:T(8,128)S(1)}, u32[]{:S(2)}, u32[]{:S(2)}) %collective-permute-start) | collective-permute-done | bytes 16416 | tf_op jit(solution)/shard_map/while/body/eval_jaxpr/ppermute | solution.py:16
  73.6 1.9 collective-permute-start
  75.5 4.3 %collective-permute-done = f32[16,256]{1,0:T(8,128)S(1)} collective-permute-done((f32[16,256]{1,0:T(8,128)S(1)}, f32[16,256]{1,0:T(8,128)S(1)}, u32[]{:S(2)}, u32[]{:S(2)}) %collective-permute-start) | collective-permute-done | bytes 16416 | tf_op jit(solution)/shard_map/while/body/eval_jaxpr/ppermute | solution.py:16
  82.2 1.9 collective-permute-start
  84.1 4.3 %collective-permute-done = f32[16,256]{1,0:T(8,128)S(1)} collective-permute-done((f32[16,256]{1,0:T(8,128)S(1)}, f32[16,256]{1,0:T(8,128)S(1)}, u32[]{:S(2)}, u32[]{:S(2)}) %collective-permute-start) | collective-permute-done | bytes 16416 | tf_op jit(solution)/shard_map/while/body/eval_jaxpr/ppermute | solution.py:16
  90.9 1.9 collective-permute-start
  92.8 4.3 %collective-permute-done = f32[16,256]{1,0:T(8,128)S(1)} collective-permute-done((f32[16,256]{1,0:T(8,128)S(1)}, f32[16,256]{1,0:T(8,128)S(1)}, u32[]{:S(2)}, u32[]{:S(2)}) %collective-permute-start) | collective-permute-done | bytes 16416 | tf_op jit(solution)/shard_map/while/body/eval_jaxpr/ppermute | solution.py:16
  99.5 1.9 collective-permute-start
  101.4 4.3 %collective-permute-done = f32[16,256]{1,0:T(8,128)S(1)} collective-permute-done((f32[16,256]{1,0:T(8,128)S(1)}, f32[16,256]{1,0:T(8,128)S(1)}, u32[]{:S(2)}, u32[]{:S(2)}) %collective-permute-start) | collective-permute-done | bytes 16416 | tf_op jit(solution)/shard_map/while/body/eval_jaxpr/ppermute | solution.py:16
  108.2 1.9 collective-permute-start
  110.1 4.3 %collective-permute-done = f32[16,256]{1,0:T(8,128)S(1)} collective-permute-done((f32[16,256]{1,0:T(8,128)S(1)}, f32[16,256]{1,0:T(8,128)S(1)}, u32[]{:S(2)}, u32[]{:S(2)}) %collective-permute-start) | collective-permute-done | bytes 16416 | tf_op jit(solution)/shard_map/while/body/eval_jaxpr/ppermute | solution.py:16
  116.8 1.9 collective-permute-start
  118.7 4.3 %collective-permute-done = f32[16,256]{1,0:T(8,128)S(1)} collective-permute-done((f32[16,256]{1,0:T(8,128)S(1)}, f32[16,256]{1,0:T(8,128)S(1)}, u32[]{:S(2)}, u32[]{:S(2)}) %collective-permute-start) | collective-permute-done | bytes 16416 | tf_op jit(solution)/shard_map/while/body/eval_jaxpr/ppermute | solution.py:16
  125.4 1.9 collective-permute-start
  127.4 4.3 %collective-permute-done = f32[16,256]{1,0:T(8,128)S(1)} collective-permute-done((f32[16,256]{1,0:T(8,128)S(1)}, f32[16,256]{1,0:T(8,128)S(1)}, u32[]{:S(2)}, u32[]{:S(2)}) %collective-permute-start) | collective-permute-done | bytes 16416 | tf_op jit(solution)/shard_map/while/body/eval_jaxpr/ppermute | solution.py:16
  134.2 64.9 %all_gather.3 = f32[16,8192]{0,1:T(8,128)} all-gather(f32[16,256]{0,1:T(8,128)S(1)} %copy.18), channel_id=1, replica_groups=mesh['grp'=16,'dev'=32] {'dev'}, dimensions={1}, use_global_device_ids=true | all-gather | bytes 540672 | tf_op jit(solution)/shard_map/all_gather | solution.py:64
  199.2 84.1 %gather_fusion = f32[24576,16]{1,0:T(8,128)} fusion(f32[16,8192]{0,1:T(8,128)} %all_gather.3, s32[24576]{0:T(1024)S(1)} %broadcast_clamp_fusion), kind=kCustom, calls=%fused_computation | custom fusion | bytes 3244032 | tf_op jit(solution)/shard_map/jit(_take)/gather | solution.py:67
  283.3 7.7 %copy.20 = f32[24,1024,16]{1,0,2:T(8,128)S(1)} copy(f32[24,1024,16]{2,1,0:T(8,128)} %bitcast.87) | data formatting | bytes 3145728 | tf_op jit(solution)/shard_map/jit(_take)/gather | solution.py:67
  291.1 1.7 fusion
  292.8 8.6 %gather_fusion.1 = f32[2048]{0:T(1024)S(1)} fusion(f32[1024]{0:T(1024)S(1)} %fusion.16, s32[2048]{0:T(1024)S(1)} %broadcast_clamp_fusion.1), kind=kCustom, calls=%fused_computation.1 | custom fusion | bytes 24576 | tf_op jit(solution)/shard_map/jit(_take)/gather | solution.py:72
  302.1 6.3 %all-to-all-start = ((f32[32,1,64]{2,1,0:T(1,128)}), f32[32,1,64]{2,1,0:T(1,128)S(1)}, u32[]{:S(2)}, u32[]{:S(2)}) async-start(f32[32,1,64]{2,1,0:T(1,128)} %and_select_fusion), calls=%async_computation | async-start | bytes 32768 | tf_op jit(solution)/shard_map/all_to_all | solution.py:73
  309.9 10.0 %fusion.23 = f32[128]{0:T(128)S(1)} fusion(f32[]{:T(128)} %bitcast.31, s32[]{:T(128)} %bitcast.32, f32[]{:T(128)} %bitcast.29, s32[]{:T(128)} %bitcast.30, f32[]{:T(128)} %bitcast.27, s32[]{:T(128)} %bitcast.28, f32[]{:T(128)} %bitcast.25, s32[]{:T(128)} %bitcast.26, f32[]{:T(128)} %bitcast.23, s32[]{:T(128)} %bitcast.24, f32[]{:T(128)} %bitcast.21, ...), kind=kLoop, calls=%fused_computation.50 | loop fusion | flops 6144 | bytes 580 | tf_op jit(solution)/shard_map/add | solution.py:95
  322.5 12.7 %scatter_custom_fusion = f32[16385]{0:T(1024)S(1)} fusion(s32[2048]{0:T(1024)S(1)} %bitcast.96, f32[2048]{0:T(1024)S(1)} %reshape.242, f32[]{:T(128)} %constant.61.clone.1), kind=kCustom, calls=%fused_computation.28 | custom fusion | flops 2048 | bytes 65544 | tf_op jit(solution)/shard_map/scatter-add | solution.py:79
  335.3 2.9 collective-permute-start.2
  338.2 5.0 %collective-permute-start.1 = (f32[3,128]{1,0:T(4,128)S(1)}, f32[3,128]{1,0:T(4,128)S(1)}, u32[]{:S(2)}, u32[]{:S(2)}) collective-permute-start(f32[3,128]{1,0:T(4,128)S(1)} %get-tuple-element.40), channel_id=1, source_target_pairs={{0,1},{1,2},{2,3},{3,4},{4,5},{5,6},{6,7},{7,8},{8,9},{9,10},{10,1... | collective-permute-start | bytes 4616 | tf_op jit(solution)/shard_map/ppermute | solution.py:27
  352.1 5.7 %fusion.11 = f32[1,1,128,128]{3,2,1,0:T(8,128)} fusion(f32[1,1,128,128]{3,2,1,0:T(8,128)S(1)} %copy-done.1, f32[134,128]{1,0:T(8,128)S(1)} %pad_maximum_fusion, s32[]{:T(128)S(6)} %select_n.103, s32[]{:T(128)S(6)} %select_n.102, s32[]{:T(128)S(6)} %select_n.101, s32[]{:T(128)S(6)} %select_n.100, s32[]{:T(128)S(6)} %select_n.99, s32[]{:T(128)S(6)} %select_n.98, ...), kind=kLoop, calls=%fused_computation.23 | loop fusion | flops 278528 | bytes 655936 | tf_op jit(solution)/shard_map/broadcast_in_dim | solution.py:97
  (66 shorter events, 35.3 us)
Async XLA Ops:
  0.6 290.4 %copy-start = (f32[24,24]{1,0:T(8,128)S(1)}, f32[24,24]{1,0:T(8,128)}, u32[]{:S(2)}) copy-start(f32[24,24]{1,0:T(8,128)} %param.17) | copy-start | bytes 6916
  4.4 6.3 %collective-permute-start = (f32[16,256]{1,0:T(8,128)S(1)}, f32[16,256]{1,0:T(8,128)S(1)}, u32[]{:S(2)}, u32[]{:S(2)}) collective-permute-start(f32[16,256]{1,0:T(8,128)S(1)} %get-tuple-element.96), channel_id=1, source_target_pairs={{0,32},{32,64},{64,96},{96,128},{128,160},{160,192},{192,224},{224... | collective-permute-start | bytes 49160 | tf_op jit(solution)/shard_map/while/body/eval_jaxpr/ppermute | solution.py:16
  13.0 6.3 %collective-permute-start = (f32[16,256]{1,0:T(8,128)S(1)}, f32[16,256]{1,0:T(8,128)S(1)}, u32[]{:S(2)}, u32[]{:S(2)}) collective-permute-start(f32[16,256]{1,0:T(8,128)S(1)} %get-tuple-element.96), channel_id=1, source_target_pairs={{0,32},{32,64},{64,96},{96,128},{128,160},{160,192},{192,224},{224... | collective-permute-start | bytes 49160 | tf_op jit(solution)/shard_map/while/body/eval_jaxpr/ppermute | solution.py:16
  21.7 6.3 %collective-permute-start = (f32[16,256]{1,0:T(8,128)S(1)}, f32[16,256]{1,0:T(8,128)S(1)}, u32[]{:S(2)}, u32[]{:S(2)}) collective-permute-start(f32[16,256]{1,0:T(8,128)S(1)} %get-tuple-element.96), channel_id=1, source_target_pairs={{0,32},{32,64},{64,96},{96,128},{128,160},{160,192},{192,224},{224... | collective-permute-start | bytes 49160 | tf_op jit(solution)/shard_map/while/body/eval_jaxpr/ppermute | solution.py:16
  30.3 6.3 %collective-permute-start = (f32[16,256]{1,0:T(8,128)S(1)}, f32[16,256]{1,0:T(8,128)S(1)}, u32[]{:S(2)}, u32[]{:S(2)}) collective-permute-start(f32[16,256]{1,0:T(8,128)S(1)} %get-tuple-element.96), channel_id=1, source_target_pairs={{0,32},{32,64},{64,96},{96,128},{128,160},{160,192},{192,224},{224... | collective-permute-start | bytes 49160 | tf_op jit(solution)/shard_map/while/body/eval_jaxpr/ppermute | solution.py:16
  39.0 6.3 %collective-permute-start = (f32[16,256]{1,0:T(8,128)S(1)}, f32[16,256]{1,0:T(8,128)S(1)}, u32[]{:S(2)}, u32[]{:S(2)}) collective-permute-start(f32[16,256]{1,0:T(8,128)S(1)} %get-tuple-element.96), channel_id=1, source_target_pairs={{0,32},{32,64},{64,96},{96,128},{128,160},{160,192},{192,224},{224... | collective-permute-start | bytes 49160 | tf_op jit(solution)/shard_map/while/body/eval_jaxpr/ppermute | solution.py:16
  47.6 6.3 %collective-permute-start = (f32[16,256]{1,0:T(8,128)S(1)}, f32[16,256]{1,0:T(8,128)S(1)}, u32[]{:S(2)}, u32[]{:S(2)}) collective-permute-start(f32[16,256]{1,0:T(8,128)S(1)} %get-tuple-element.96), channel_id=1, source_target_pairs={{0,32},{32,64},{64,96},{96,128},{128,160},{160,192},{192,224},{224... | collective-permute-start | bytes 49160 | tf_op jit(solution)/shard_map/while/body/eval_jaxpr/ppermute | solution.py:16
  56.3 6.3 %collective-permute-start = (f32[16,256]{1,0:T(8,128)S(1)}, f32[16,256]{1,0:T(8,128)S(1)}, u32[]{:S(2)}, u32[]{:S(2)}) collective-permute-start(f32[16,256]{1,0:T(8,128)S(1)} %get-tuple-element.96), channel_id=1, source_target_pairs={{0,32},{32,64},{64,96},{96,128},{128,160},{160,192},{192,224},{224... | collective-permute-start | bytes 49160 | tf_op jit(solution)/shard_map/while/body/eval_jaxpr/ppermute | solution.py:16
  64.9 6.3 %collective-permute-start = (f32[16,256]{1,0:T(8,128)S(1)}, f32[16,256]{1,0:T(8,128)S(1)}, u32[]{:S(2)}, u32[]{:S(2)}) collective-permute-start(f32[16,256]{1,0:T(8,128)S(1)} %get-tuple-element.96), channel_id=1, source_target_pairs={{0,32},{32,64},{64,96},{96,128},{128,160},{160,192},{192,224},{224... | collective-permute-start | bytes 49160 | tf_op jit(solution)/shard_map/while/body/eval_jaxpr/ppermute | solution.py:16
  73.6 6.3 %collective-permute-start = (f32[16,256]{1,0:T(8,128)S(1)}, f32[16,256]{1,0:T(8,128)S(1)}, u32[]{:S(2)}, u32[]{:S(2)}) collective-permute-start(f32[16,256]{1,0:T(8,128)S(1)} %get-tuple-element.96), channel_id=1, source_target_pairs={{0,32},{32,64},{64,96},{96,128},{128,160},{160,192},{192,224},{224... | collective-permute-start | bytes 49160 | tf_op jit(solution)/shard_map/while/body/eval_jaxpr/ppermute | solution.py:16
  82.2 6.3 %collective-permute-start = (f32[16,256]{1,0:T(8,128)S(1)}, f32[16,256]{1,0:T(8,128)S(1)}, u32[]{:S(2)}, u32[]{:S(2)}) collective-permute-start(f32[16,256]{1,0:T(8,128)S(1)} %get-tuple-element.96), channel_id=1, source_target_pairs={{0,32},{32,64},{64,96},{96,128},{128,160},{160,192},{192,224},{224... | collective-permute-start | bytes 49160 | tf_op jit(solution)/shard_map/while/body/eval_jaxpr/ppermute | solution.py:16
  90.9 6.3 %collective-permute-start = (f32[16,256]{1,0:T(8,128)S(1)}, f32[16,256]{1,0:T(8,128)S(1)}, u32[]{:S(2)}, u32[]{:S(2)}) collective-permute-start(f32[16,256]{1,0:T(8,128)S(1)} %get-tuple-element.96), channel_id=1, source_target_pairs={{0,32},{32,64},{64,96},{96,128},{128,160},{160,192},{192,224},{224... | collective-permute-start | bytes 49160 | tf_op jit(solution)/shard_map/while/body/eval_jaxpr/ppermute | solution.py:16
  99.5 6.3 %collective-permute-start = (f32[16,256]{1,0:T(8,128)S(1)}, f32[16,256]{1,0:T(8,128)S(1)}, u32[]{:S(2)}, u32[]{:S(2)}) collective-permute-start(f32[16,256]{1,0:T(8,128)S(1)} %get-tuple-element.96), channel_id=1, source_target_pairs={{0,32},{32,64},{64,96},{96,128},{128,160},{160,192},{192,224},{224... | collective-permute-start | bytes 49160 | tf_op jit(solution)/shard_map/while/body/eval_jaxpr/ppermute | solution.py:16
  108.2 6.3 %collective-permute-start = (f32[16,256]{1,0:T(8,128)S(1)}, f32[16,256]{1,0:T(8,128)S(1)}, u32[]{:S(2)}, u32[]{:S(2)}) collective-permute-start(f32[16,256]{1,0:T(8,128)S(1)} %get-tuple-element.96), channel_id=1, source_target_pairs={{0,32},{32,64},{64,96},{96,128},{128,160},{160,192},{192,224},{224... | collective-permute-start | bytes 49160 | tf_op jit(solution)/shard_map/while/body/eval_jaxpr/ppermute | solution.py:16
  116.8 6.3 %collective-permute-start = (f32[16,256]{1,0:T(8,128)S(1)}, f32[16,256]{1,0:T(8,128)S(1)}, u32[]{:S(2)}, u32[]{:S(2)}) collective-permute-start(f32[16,256]{1,0:T(8,128)S(1)} %get-tuple-element.96), channel_id=1, source_target_pairs={{0,32},{32,64},{64,96},{96,128},{128,160},{160,192},{192,224},{224... | collective-permute-start | bytes 49160 | tf_op jit(solution)/shard_map/while/body/eval_jaxpr/ppermute | solution.py:16
  125.4 6.3 %collective-permute-start = (f32[16,256]{1,0:T(8,128)S(1)}, f32[16,256]{1,0:T(8,128)S(1)}, u32[]{:S(2)}, u32[]{:S(2)}) collective-permute-start(f32[16,256]{1,0:T(8,128)S(1)} %get-tuple-element.96), channel_id=1, source_target_pairs={{0,32},{32,64},{64,96},{96,128},{128,160},{160,192},{192,224},{224... | collective-permute-start | bytes 49160 | tf_op jit(solution)/shard_map/while/body/eval_jaxpr/ppermute | solution.py:16
  134.1 65.0 %copy-start.2 = (f32[16,256]{1,0:T(8,128)}, f32[16,256]{1,0:T(8,128)S(1)}, u32[]{:S(2)}) copy-start(f32[16,256]{1,0:T(8,128)S(1)} %get-tuple-element.29) | copy-start | bytes 49156
  283.3 7.7 %copy-start.3 = (s32[1,1,32,64]{3,2,1,0:T(8,128)S(1)}, s32[1,1,32,64]{3,2,1,0:T(8,128)}, u32[]{:S(2)}) copy-start(s32[1,1,32,64]{3,2,1,0:T(8,128)} %param.21) | copy-start | bytes 24580
  290.9 1.8 copy-start.7
  292.8 15.7 %copy-start.6 = (s32[1,1,32,64]{3,2,1,0:T(8,128)S(1)}, s32[1,1,32,64]{3,2,1,0:T(8,128)}, u32[]{:S(2)}) copy-start(s32[1,1,32,64]{3,2,1,0:T(8,128)} %param.22) | copy-start | bytes 24580
  292.8 15.8 %copy-start.4 = (s32[8]{0:T(128)S(1)}, s32[8]{0:T(128)}, u32[]{:S(2)}) copy-start(s32[8]{0:T(128)} %param.24) | copy-start | bytes 100
  292.8 16.5 %copy-start.5 = (f32[8]{0:T(128)S(1)}, f32[8]{0:T(128)}, u32[]{:S(2)}) copy-start(f32[8]{0:T(128)} %param.25) | copy-start | bytes 100
  292.8 42.4 %copy-start.1 = (f32[1,1,128,128]{3,2,1,0:T(8,128)S(1)}, f32[1,1,128,128]{3,2,1,0:T(8,128)}, u32[]{:S(2)}) copy-start(f32[1,1,128,128]{3,2,1,0:T(8,128)} %param.23) | copy-start | bytes 196612
  302.1 19.0 %all-to-all-start = ((f32[32,1,64]{2,1,0:T(1,128)}), f32[32,1,64]{2,1,0:T(1,128)S(1)}, u32[]{:S(2)}, u32[]{:S(2)}) async-start(f32[32,1,64]{2,1,0:T(1,128)} %and_select_fusion), calls=%async_computation | async-start | bytes 32768 | tf_op jit(solution)/shard_map/all_to_all | solution.py:73
  335.3 16.8 %collective-permute-start.2 = (f32[3,128]{1,0:T(4,128)S(1)}, f32[3,128]{1,0:T(4,128)S(1)}, u32[]{:S(2)}, u32[]{:S(2)}) collective-permute-start(f32[3,128]{1,0:T(4,128)S(1)} %get-tuple-element.41), channel_id=1, source_target_pairs={{1,0},{2,1},{3,2},{4,3},{5,4},{6,5},{7,6},{8,7},{9,8},{10,9},{11,1... | collective-permute-start | bytes 4616 | tf_op jit(solution)/shard_map/ppermute | solution.py:29
  338.2 13.8 %collective-permute-start.1 = (f32[3,128]{1,0:T(4,128)S(1)}, f32[3,128]{1,0:T(4,128)S(1)}, u32[]{:S(2)}, u32[]{:S(2)}) collective-permute-start(f32[3,128]{1,0:T(4,128)S(1)} %get-tuple-element.40), channel_id=1, source_target_pairs={{0,1},{1,2},{2,3},{3,4},{4,5},{5,6},{6,7},{7,8},{8,9},{9,10},{10,1... | collective-permute-start | bytes 4616 | tf_op jit(solution)/shard_map/ppermute | solution.py:27
where the time goes:
time: 360 us; the launch traced here: 358 us
  local copies, waits for them, and re-layouts  103 us (29%)
  waiting for transfers between devices  65.1 us (18%)
  blocking collectives  64.9 us (18%)
  starting transfers between devices  43.1 us (12%)
  matrix products  37.8 us (10%)
  other arithmetic  32.4 us (9%)
  between operations  10.9 us (3%)
    gather x2, local copies, waits for them, and re-layouts, on_device(): motion = jnp.take(columns, lookup, axis=1)  91.8 us
    ppermute x15, waiting for transfers between devices, passed_along(): lax.ppermute(value, axis, [(source, source + steps) for source in range(l...  65.1 us
    all_gather x1, blocking collectives, on_device(): columns = lax.all_gather(solved, 'dev', axis=1, tiled=True)  64.9 us
    dot_general x31, matrix products, product(): jnp.dot(left, right, precision=exact_mode, preferred_element_type=jnp.flo...  36.1 us
    ppermute x15, starting transfers between devices, passed_along(): lax.ppermute(value, axis, [(source, source + steps) for source in range(l...  28.8 us
    scatter-add x1, other arithmetic, on_device(): jax.ops.segment_sum(received.ravel(), segment_ids.ravel(), num_segments=c...  12.7 us
    add x1, other arithmetic, on_device(): weight_sum = weight_sum + filter_weights[which] * inside  10 us
    gather x2, local copies, waits for them, and re-layouts, on_device(): outgoing = jnp.take(sensitivity, send_elements[0, 0], axis=0)  8.67 us
  transfers between devices with their start and end apart: 18, of which 15 were waited for; matrix products, arithmetic and copies ran while one was open for 3% of the time, Pallas kernels for 0%

commit v1 on v0

--- a/solution.py
+++ b/solution.py
@@ -61,7 +61,10 @@
         return product(rights - product(previous, couple), inverse)
 
     solved = lax.fori_loop(0, lax.axis_size("grp") - 1, advance, source)
-    columns = lax.all_gather(solved, "dev", axis=1, tiled=True)
+    n_dev = lax.axis_size("dev")
+    pieces = jnp.stack([solved for _ in range(n_dev)])
+    pieces = lax.all_to_all(pieces, "dev", split_axis=0, concat_axis=0)
+    columns = jnp.concatenate(pieces, axis=1)
     panel_order = solved.shape[1]
     lookup = element_substructure[0, 0][None, :] * panel_order + element_rows[0, 0]
     motion = jnp.take(columns, lookup, axis=1)

time: 360 us -> 320 us (0.89)
  blocking collectives: 64.9 us -> 0 us
  starting transfers between devices: 43.1 us -> 55.7 us
  waiting for transfers between devices: 65.1 us -> 77.2 us
    all_gather x1 -> x0, blocking collectives: 64.9 us -> none  [on_device(): columns = lax.all_gather(solved, 'dev', axis=1, tiled=True)]
    all_to_all x0 -> x1, starting transfers between devices: none -> 13.4 us  [on_device(): pieces = lax.all_to_all(pieces, 'dev', split_axis=0, concat_axis=0)]
    all_to_all x0 -> x1, waiting for transfers between devices: none -> 12.1 us  [on_device(): pieces = lax.all_to_all(pieces, 'dev', split_axis=0, concat_axis=0)]
  transfers between devices with their start and end apart: 18 -> 19, of which waited for: 15 -> 16; matrix products, arithmetic and copies ran while one was open for 3% -> 4% of each run, Pallas kernels for 0% -> 0%
where the time goes in v1:
time: 320 us; the launch traced here: 318 us
  local copies, waits for them, and re-layouts  106 us (33%)
  waiting for transfers between devices  77.2 us (24%)
  starting transfers between devices  55.7 us (17%)
  matrix products  37.8 us (12%)
  other arithmetic  30.1 us (9%)
  between operations  10.7 us (3%)
    gather x2, local copies, waits for them, and re-layouts, on_device(): motion = jnp.take(columns, lookup, axis=1)  91.7 us
    ppermute x15, waiting for transfers between devices, passed_along(): lax.ppermute(value, axis, [(source, source + steps) for source in range(l...  65.1 us
    dot_general x31, matrix products, product(): jnp.dot(left, right, precision=exact_mode, preferred_element_type=jnp.flo...  36.1 us
    ppermute x15, starting transfers between devices, passed_along(): lax.ppermute(value, axis, [(source, source + steps) for source in range(l...  28.8 us
    all_to_all x1, starting transfers between devices, on_device(): pieces = lax.all_to_all(pieces, 'dev', split_axis=0, concat_axis=0)  13.4 us
    scatter-add x1, other arithmetic, on_device(): jax.ops.segment_sum(received.ravel(), segment_ids.ravel(), num_segments=c...  12.7 us
    all_to_all x1, waiting for transfers between devices, on_device(): pieces = lax.all_to_all(pieces, 'dev', split_axis=0, concat_axis=0)  12.1 us
    add x1, other arithmetic, on_device(): weight_sum = weight_sum + filter_weights[which] * inside  10 us
  transfers between devices with their start and end apart: 19, of which 16 were waited for; matrix products, arithmetic and copies ran while one was open for 4% of the time, Pallas kernels for 0%

profile of v1, /device:TPU:38, one launch (start us, length us, event | category | flops | bytes accessed | tf_op | source)
XLA Modules:
  0.0 318.4 jit_solution(12566488111940631395)
XLA Ops:
  1.8 129.7 %while.10 = (s32[]{:T(128)}, f32[16,256]{1,0:T(8,128)S(1)}, f32[256,256]{1,0:T(8,128)}, f32[16,256]{1,0:T(8,128)}, f32[256,256]{1,0:T(8,128)}, /*index=5*/s32[]{:T(128)}) while((s32[]{:T(128)}, f32[16,256]{1,0:T(8,128)S(1)}, f32[256,256]{1,0:T(8,128)}, f32[16,256]{1,0:T(8,128)}, f32[256,256]{1,0:T(8,128)}, /*index=5*/s32[]{:T(128)}) %tuple.42), condition=%wide.region_1.0_spmd, body=%wide.region_0.0_spmd.sunk | while | flops 25169920 | bytes 671853 | solution.py:63
  1.8 1.9 collective-permute-start
  3.8 4.3 %collective-permute-done = f32[16,256]{1,0:T(8,128)S(1)} collective-permute-done((f32[16,256]{1,0:T(8,128)S(1)}, f32[16,256]{1,0:T(8,128)S(1)}, u32[]{:S(2)}, u32[]{:S(2)}) %collective-permute-start) | collective-permute-done | bytes 16416 | tf_op jit(solution)/shard_map/while/body/eval_jaxpr/ppermute | solution.py:16
  8.1 1.2 convolution_subtract_fusion.2
  10.5 1.9 collective-permute-start
  12.4 4.3 %collective-permute-done = f32[16,256]{1,0:T(8,128)S(1)} collective-permute-done((f32[16,256]{1,0:T(8,128)S(1)}, f32[16,256]{1,0:T(8,128)S(1)}, u32[]{:S(2)}, u32[]{:S(2)}) %collective-permute-start) | collective-permute-done | bytes 16416 | tf_op jit(solution)/shard_map/while/body/eval_jaxpr/ppermute | solution.py:16
  16.8 1.2 convolution_subtract_fusion.2
  19.1 1.9 collective-permute-start
  21.1 4.3 %collective-permute-done = f32[16,256]{1,0:T(8,128)S(1)} collective-permute-done((f32[16,256]{1,0:T(8,128)S(1)}, f32[16,256]{1,0:T(8,128)S(1)}, u32[]{:S(2)}, u32[]{:S(2)}) %collective-permute-start) | collective-permute-done | bytes 16416 | tf_op jit(solution)/shard_map/while/body/eval_jaxpr/ppermute | solution.py:16
  25.4 1.2 convolution_subtract_fusion.2
  27.8 1.9 collective-permute-start
  29.7 4.3 %collective-permute-done = f32[16,256]{1,0:T(8,128)S(1)} collective-permute-done((f32[16,256]{1,0:T(8,128)S(1)}, f32[16,256]{1,0:T(8,128)S(1)}, u32[]{:S(2)}, u32[]{:S(2)}) %collective-permute-start) | collective-permute-done | bytes 16416 | tf_op jit(solution)/shard_map/while/body/eval_jaxpr/ppermute | solution.py:16
  34.1 1.2 convolution_subtract_fusion.2
  36.4 1.9 collective-permute-start
  38.4 4.3 %collective-permute-done = f32[16,256]{1,0:T(8,128)S(1)} collective-permute-done((f32[16,256]{1,0:T(8,128)S(1)}, f32[16,256]{1,0:T(8,128)S(1)}, u32[]{:S(2)}, u32[]{:S(2)}) %collective-permute-start) | collective-permute-done | bytes 16416 | tf_op jit(solution)/shard_map/while/body/eval_jaxpr/ppermute | solution.py:16
  45.1 1.9 collective-permute-start
  47.0 4.3 %collective-permute-done = f32[16,256]{1,0:T(8,128)S(1)} collective-permute-done((f32[16,256]{1,0:T(8,128)S(1)}, f32[16,256]{1,0:T(8,128)S(1)}, u32[]{:S(2)}, u32[]{:S(2)}) %collective-permute-start) | collective-permute-done | bytes 16416 | tf_op jit(solution)/shard_map/while/body/eval_jaxpr/ppermute | solution.py:16
  53.7 1.9 collective-permute-start
  55.7 4.3 %collective-permute-done = f32[16,256]{1,0:T(8,128)S(1)} collective-permute-done((f32[16,256]{1,0:T(8,128)S(1)}, f32[16,256]{1,0:T(8,128)S(1)}, u32[]{:S(2)}, u32[]{:S(2)}) %collective-permute-start) | collective-permute-done | bytes 16416 | tf_op jit(solution)/shard_map/while/body/eval_jaxpr/ppermute | solution.py:16
  62.4 1.9 collective-permute-start
  64.3 4.3 %collective-permute-done = f32[16,256]{1,0:T(8,128)S(1)} collective-permute-done((f32[16,256]{1,0:T(8,128)S(1)}, f32[16,256]{1,0:T(8,128)S(1)}, u32[]{:S(2)}, u32[]{:S(2)}) %collective-permute-start) | collective-permute-done | bytes 16416 | tf_op jit(solution)/shard_map/while/body/eval_jaxpr/ppermute | solution.py:16
  71.0 1.9 collective-permute-start
  73.0 4.3 %collective-permute-done = f32[16,256]{1,0:T(8,128)S(1)} collective-permute-done((f32[16,256]{1,0:T(8,128)S(1)}, f32[16,256]{1,0:T(8,128)S(1)}, u32[]{:S(2)}, u32[]{:S(2)}) %collective-permute-start) | collective-permute-done | bytes 16416 | tf_op jit(solution)/shard_map/while/body/eval_jaxpr/ppermute | solution.py:16
  79.7 1.9 collective-permute-start
  81.6 4.3 %collective-permute-done = f32[16,256]{1,0:T(8,128)S(1)} collective-permute-done((f32[16,256]{1,0:T(8,128)S(1)}, f32[16,256]{1,0:T(8,128)S(1)}, u32[]{:S(2)}, u32[]{:S(2)}) %collective-permute-start) | collective-permute-done | bytes 16416 | tf_op jit(solution)/shard_map/while/body/eval_jaxpr/ppermute | solution.py:16
  88.3 1.9 collective-permute-start
  90.2 4.3 %collective-permute-done = f32[16,256]{1,0:T(8,128)S(1)} collective-permute-done((f32[16,256]{1,0:T(8,128)S(1)}, f32[16,256]{1,0:T(8,128)S(1)}, u32[]{:S(2)}, u32[]{:S(2)}) %collective-permute-start) | collective-permute-done | bytes 16416 | tf_op jit(solution)/shard_map/while/body/eval_jaxpr/ppermute | solution.py:16
  97.0 1.9 collective-permute-start
  98.9 4.3 %collective-permute-done = f32[16,256]{1,0:T(8,128)S(1)} collective-permute-done((f32[16,256]{1,0:T(8,128)S(1)}, f32[16,256]{1,0:T(8,128)S(1)}, u32[]{:S(2)}, u32[]{:S(2)}) %collective-permute-start) | collective-permute-done | bytes 16416 | tf_op jit(solution)/shard_map/while/body/eval_jaxpr/ppermute | solution.py:16
  105.6 1.9 collective-permute-start
  107.5 4.3 %collective-permute-done = f32[16,256]{1,0:T(8,128)S(1)} collective-permute-done((f32[16,256]{1,0:T(8,128)S(1)}, f32[16,256]{1,0:T(8,128)S(1)}, u32[]{:S(2)}, u32[]{:S(2)}) %collective-permute-start) | collective-permute-done | bytes 16416 | tf_op jit(solution)/shard_map/while/body/eval_jaxpr/ppermute | solution.py:16
  114.3 1.9 collective-permute-start
  116.2 4.3 %collective-permute-done = f32[16,256]{1,0:T(8,128)S(1)} collective-permute-done((f32[16,256]{1,0:T(8,128)S(1)}, f32[16,256]{1,0:T(8,128)S(1)}, u32[]{:S(2)}, u32[]{:S(2)}) %collective-permute-start) | collective-permute-done | bytes 16416 | tf_op jit(solution)/shard_map/while/body/eval_jaxpr/ppermute | solution.py:16
  122.9 1.9 collective-permute-start
  124.8 4.3 %collective-permute-done = f32[16,256]{1,0:T(8,128)S(1)} collective-permute-done((f32[16,256]{1,0:T(8,128)S(1)}, f32[16,256]{1,0:T(8,128)S(1)}, u32[]{:S(2)}, u32[]{:S(2)}) %collective-permute-start) | collective-permute-done | bytes 16416 | tf_op jit(solution)/shard_map/while/body/eval_jaxpr/ppermute | solution.py:16
  132.5 13.4 %all-to-all-start = ((f32[32,16,256]{2,1,0:T(8,128)}), f32[32,16,256]{2,1,0:T(8,128)S(1)}, u32[]{:S(2)}, u32[]{:S(2)}) async-start(f32[32,16,256]{2,1,0:T(8,128)} %stack.2), calls=%async_computation | async-start | bytes 1048576 | tf_op jit(solution)/shard_map/all_to_all | solution.py:66
  147.6 12.1 %all-to-all-done = f32[32,16,256]{2,1,0:T(8,128)S(1)} async-done(((f32[32,16,256]{2,1,0:T(8,128)}), f32[32,16,256]{2,1,0:T(8,128)S(1)}, u32[]{:S(2)}, u32[]{:S(2)}) %all-to-all-start) | async-done | bytes 524320 | tf_op jit(solution)/shard_map/all_to_all | solution.py:66
  159.7 2.6 copy.18
  162.3 84.0 %gather_fusion = f32[24576,16]{1,0:T(8,128)} fusion(f32[16,8192]{0,1:T(8,128)} %bitcast.89, s32[24576]{0:T(1024)S(1)} %broadcast_clamp_fusion), kind=kCustom, calls=%fused_computation | custom fusion | bytes 3244032 | tf_op jit(solution)/shard_map/jit(_take)/gather | solution.py:70
  246.4 7.6 %copy.20 = f32[24,1024,16]{1,0,2:T(8,128)S(1)} copy(f32[24,1024,16]{2,1,0:T(8,128)} %bitcast.90) | data formatting | bytes 3145728 | tf_op jit(solution)/shard_map/jit(_take)/gather | solution.py:70
  254.0 1.7 fusion
  255.8 8.6 %gather_fusion.1 = f32[2048]{0:T(1024)S(1)} fusion(f32[1024]{0:T(1024)S(1)} %fusion.16, s32[2048]{0:T(1024)S(1)} %broadcast_clamp_fusion.1), kind=kCustom, calls=%fused_computation.1 | custom fusion | bytes 24576 | tf_op jit(solution)/shard_map/jit(_take)/gather | solution.py:75
  265.1 5.6 %all-to-all-start.1 = ((f32[32,1,64]{2,1,0:T(1,128)}), f32[32,1,64]{2,1,0:T(1,128)S(1)}, u32[]{:S(2)}, u32[]{:S(2)}) async-start(f32[32,1,64]{2,1,0:T(1,128)} %and_select_fusion), calls=%async_computation.1 | async-start | bytes 32768 | tf_op jit(solution)/shard_map/all_to_all | solution.py:76
  270.7 10.0 %fusion.23 = f32[128]{0:T(128)S(1)} fusion(f32[]{:T(128)} %bitcast.33, s32[]{:T(128)} %bitcast.34, f32[]{:T(128)} %bitcast.31, s32[]{:T(128)} %bitcast.32, f32[]{:T(128)} %bitcast.29, s32[]{:T(128)} %bitcast.30, f32[]{:T(128)} %bitcast.27, s32[]{:T(128)} %bitcast.28, f32[]{:T(128)} %bitcast.25, s32[]{:T(128)} %bitcast.26, f32[]{:T(128)} %bitcast.23, ...), kind=kLoop, calls=%fused_computation.50 | loop fusion | flops 6144 | bytes 580 | tf_op jit(solution)/shard_map/add | solution.py:98
  283.1 12.7 %scatter_custom_fusion = f32[16385]{0:T(1024)S(1)} fusion(s32[2048]{0:T(1024)S(1)} %bitcast.100, f32[2048]{0:T(1024)S(1)} %reshape.252, f32[]{:T(128)} %constant.61.clone.1), kind=kCustom, calls=%fused_computation.28 | custom fusion | flops 2048 | bytes 65544 | tf_op jit(solution)/shard_map/scatter-add | solution.py:82
  295.8 2.9 collective-permute-start.2
  298.8 5.0 %collective-permute-start.1 = (f32[3,128]{1,0:T(4,128)S(1)}, f32[3,128]{1,0:T(4,128)S(1)}, u32[]{:S(2)}, u32[]{:S(2)}) collective-permute-start(f32[3,128]{1,0:T(4,128)S(1)} %get-tuple-element.40), channel_id=1, source_target_pairs={{0,1},{1,2},{2,3},{3,4},{4,5},{5,6},{6,7},{7,8},{8,9},{9,10},{10,1... | collective-permute-start | bytes 4616 | tf_op jit(solution)/shard_map/ppermute | solution.py:27
  312.5 5.9 %fusion.11 = f32[1,1,128,128]{3,2,1,0:T(8,128)} fusion(f32[1,1,128,128]{3,2,1,0:T(8,128)S(1)} %copy-done.2, f32[134,128]{1,0:T(8,128)S(1)} %pad_maximum_fusion, s32[]{:T(128)S(6)} %select_n.103, s32[]{:T(128)S(6)} %select_n.102, s32[]{:T(128)S(6)} %select_n.101, s32[]{:T(128)S(6)} %select_n.100, s32[]{:T(128)S(6)} %select_n.99, s32[]{:T(128)S(6)} %select_n.98, ...), kind=kLoop, calls=%fused_computation.23 | loop fusion | flops 278528 | bytes 655936 | tf_op jit(solution)/shard_map/broadcast_in_dim | solution.py:100
  (72 shorter events, 36.0 us)
Async XLA Ops:
  0.6 253.4 %copy-start = (f32[24,24]{1,0:T(8,128)S(1)}, f32[24,24]{1,0:T(8,128)}, u32[]{:S(2)}) copy-start(f32[24,24]{1,0:T(8,128)} %param.17) | copy-start | bytes 6916
  1.8 6.3 %collective-permute-start = (f32[16,256]{1,0:T(8,128)S(1)}, f32[16,256]{1,0:T(8,128)S(1)}, u32[]{:S(2)}, u32[]{:S(2)}) collective-permute-start(f32[16,256]{1,0:T(8,128)S(1)} %get-tuple-element.96), channel_id=1, source_target_pairs={{0,32},{32,64},{64,96},{96,128},{128,160},{160,192},{192,224},{224... | collective-permute-start | bytes 49160 | tf_op jit(solution)/shard_map/while/body/eval_jaxpr/ppermute | solution.py:16
  10.5 6.3 %collective-permute-start = (f32[16,256]{1,0:T(8,128)S(1)}, f32[16,256]{1,0:T(8,128)S(1)}, u32[]{:S(2)}, u32[]{:S(2)}) collective-permute-start(f32[16,256]{1,0:T(8,128)S(1)} %get-tuple-element.96), channel_id=1, source_target_pairs={{0,32},{32,64},{64,96},{96,128},{128,160},{160,192},{192,224},{224... | collective-permute-start | bytes 49160 | tf_op jit(solution)/shard_map/while/body/eval_jaxpr/ppermute | solution.py:16
  19.1 6.3 %collective-permute-start = (f32[16,256]{1,0:T(8,128)S(1)}, f32[16,256]{1,0:T(8,128)S(1)}, u32[]{:S(2)}, u32[]{:S(2)}) collective-permute-start(f32[16,256]{1,0:T(8,128)S(1)} %get-tuple-element.96), channel_id=1, source_target_pairs={{0,32},{32,64},{64,96},{96,128},{128,160},{160,192},{192,224},{224... | collective-permute-start | bytes 49160 | tf_op jit(solution)/shard_map/while/body/eval_jaxpr/ppermute | solution.py:16
  27.8 6.3 %collective-permute-start = (f32[16,256]{1,0:T(8,128)S(1)}, f32[16,256]{1,0:T(8,128)S(1)}, u32[]{:S(2)}, u32[]{:S(2)}) collective-permute-start(f32[16,256]{1,0:T(8,128)S(1)} %get-tuple-element.96), channel_id=1, source_target_pairs={{0,32},{32,64},{64,96},{96,128},{128,160},{160,192},{192,224},{224... | collective-permute-start | bytes 49160 | tf_op jit(solution)/shard_map/while/body/eval_jaxpr/ppermute | solution.py:16
  36.4 6.3 %collective-permute-start = (f32[16,256]{1,0:T(8,128)S(1)}, f32[16,256]{1,0:T(8,128)S(1)}, u32[]{:S(2)}, u32[]{:S(2)}) collective-permute-start(f32[16,256]{1,0:T(8,128)S(1)} %get-tuple-element.96), channel_id=1, source_target_pairs={{0,32},{32,64},{64,96},{96,128},{128,160},{160,192},{192,224},{224... | collective-permute-start | bytes 49160 | tf_op jit(solution)/shard_map/while/body/eval_jaxpr/ppermute | solution.py:16
  45.1 6.3 %collective-permute-start = (f32[16,256]{1,0:T(8,128)S(1)}, f32[16,256]{1,0:T(8,128)S(1)}, u32[]{:S(2)}, u32[]{:S(2)}) collective-permute-start(f32[16,256]{1,0:T(8,128)S(1)} %get-tuple-element.96), channel_id=1, source_target_pairs={{0,32},{32,64},{64,96},{96,128},{128,160},{160,192},{192,224},{224... | collective-permute-start | bytes 49160 | tf_op jit(solution)/shard_map/while/body/eval_jaxpr/ppermute | solution.py:16
  53.7 6.3 %collective-permute-start = (f32[16,256]{1,0:T(8,128)S(1)}, f32[16,256]{1,0:T(8,128)S(1)}, u32[]{:S(2)}, u32[]{:S(2)}) collective-permute-start(f32[16,256]{1,0:T(8,128)S(1)} %get-tuple-element.96), channel_id=1, source_target_pairs={{0,32},{32,64},{64,96},{96,128},{128,160},{160,192},{192,224},{224... | collective-permute-start | bytes 49160 | tf_op jit(solution)/shard_map/while/body/eval_jaxpr/ppermute | solution.py:16
  62.4 6.3 %collective-permute-start = (f32[16,256]{1,0:T(8,128)S(1)}, f32[16,256]{1,0:T(8,128)S(1)}, u32[]{:S(2)}, u32[]{:S(2)}) collective-permute-start(f32[16,256]{1,0:T(8,128)S(1)} %get-tuple-element.96), channel_id=1, source_target_pairs={{0,32},{32,64},{64,96},{96,128},{128,160},{160,192},{192,224},{224... | collective-permute-start | bytes 49160 | tf_op jit(solution)/shard_map/while/body/eval_jaxpr/ppermute | solution.py:16
  71.0 6.3 %collective-permute-start = (f32[16,256]{1,0:T(8,128)S(1)}, f32[16,256]{1,0:T(8,128)S(1)}, u32[]{:S(2)}, u32[]{:S(2)}) collective-permute-start(f32[16,256]{1,0:T(8,128)S(1)} %get-tuple-element.96), channel_id=1, source_target_pairs={{0,32},{32,64},{64,96},{96,128},{128,160},{160,192},{192,224},{224... | collective-permute-start | bytes 49160 | tf_op jit(solution)/shard_map/while/body/eval_jaxpr/ppermute | solution.py:16
  79.7 6.3 %collective-permute-start = (f32[16,256]{1,0:T(8,128)S(1)}, f32[16,256]{1,0:T(8,128)S(1)}, u32[]{:S(2)}, u32[]{:S(2)}) collective-permute-start(f32[16,256]{1,0:T(8,128)S(1)} %get-tuple-element.96), channel_id=1, source_target_pairs={{0,32},{32,64},{64,96},{96,128},{128,160},{160,192},{192,224},{224... | collective-permute-start | bytes 49160 | tf_op jit(solution)/shard_map/while/body/eval_jaxpr/ppermute | solution.py:16
  88.3 6.3 %collective-permute-start = (f32[16,256]{1,0:T(8,128)S(1)}, f32[16,256]{1,0:T(8,128)S(1)}, u32[]{:S(2)}, u32[]{:S(2)}) collective-permute-start(f32[16,256]{1,0:T(8,128)S(1)} %get-tuple-element.96), channel_id=1, source_target_pairs={{0,32},{32,64},{64,96},{96,128},{128,160},{160,192},{192,224},{224... | collective-permute-start | bytes 49160 | tf_op jit(solution)/shard_map/while/body/eval_jaxpr/ppermute | solution.py:16
  97.0 6.3 %collective-permute-start = (f32[16,256]{1,0:T(8,128)S(1)}, f32[16,256]{1,0:T(8,128)S(1)}, u32[]{:S(2)}, u32[]{:S(2)}) collective-permute-start(f32[16,256]{1,0:T(8,128)S(1)} %get-tuple-element.96), channel_id=1, source_target_pairs={{0,32},{32,64},{64,96},{96,128},{128,160},{160,192},{192,224},{224... | collective-permute-start | bytes 49160 | tf_op jit(solution)/shard_map/while/body/eval_jaxpr/ppermute | solution.py:16
  105.6 6.3 %collective-permute-start = (f32[16,256]{1,0:T(8,128)S(1)}, f32[16,256]{1,0:T(8,128)S(1)}, u32[]{:S(2)}, u32[]{:S(2)}) collective-permute-start(f32[16,256]{1,0:T(8,128)S(1)} %get-tuple-element.96), channel_id=1, source_target_pairs={{0,32},{32,64},{64,96},{96,128},{128,160},{160,192},{192,224},{224... | collective-permute-start | bytes 49160 | tf_op jit(solution)/shard_map/while/body/eval_jaxpr/ppermute | solution.py:16
  114.3 6.3 %collective-permute-start = (f32[16,256]{1,0:T(8,128)S(1)}, f32[16,256]{1,0:T(8,128)S(1)}, u32[]{:S(2)}, u32[]{:S(2)}) collective-permute-start(f32[16,256]{1,0:T(8,128)S(1)} %get-tuple-element.96), channel_id=1, source_target_pairs={{0,32},{32,64},{64,96},{96,128},{128,160},{160,192},{192,224},{224... | collective-permute-start | bytes 49160 | tf_op jit(solution)/shard_map/while/body/eval_jaxpr/ppermute | solution.py:16
  122.9 6.3 %collective-permute-start = (f32[16,256]{1,0:T(8,128)S(1)}, f32[16,256]{1,0:T(8,128)S(1)}, u32[]{:S(2)}, u32[]{:S(2)}) collective-permute-start(f32[16,256]{1,0:T(8,128)S(1)} %get-tuple-element.96), channel_id=1, source_target_pairs={{0,32},{32,64},{64,96},{96,128},{128,160},{160,192},{192,224},{224... | collective-permute-start | bytes 49160 | tf_op jit(solution)/shard_map/while/body/eval_jaxpr/ppermute | solution.py:16
  131.6 30.8 %copy-start.3 = (f32[16,256]{1,0:T(8,128)}, f32[16,256]{1,0:T(8,128)S(1)}, u32[]{:S(2)}) copy-start(f32[16,256]{1,0:T(8,128)S(1)} %get-tuple-element.29) | copy-start | bytes 49156
  131.6 14.4 %copy-start.9 = (s32[1,1,1024]{2,1,0:T(1,128)S(1)}, s32[1,1,1024]{2,1,0:T(1,128)}, u32[]{:S(2)}) copy-start(s32[1,1,1024]{2,1,0:T(1,128)} %param.18) | copy-start | bytes 12292
  131.6 14.4 %copy-start.1 = (s32[1,1,24,1024]{3,2,1,0:T(8,128)S(1)}, s32[1,1,24,1024]{3,2,1,0:T(8,128)}, u32[]{:S(2)}) copy-start(s32[1,1,24,1024]{3,2,1,0:T(8,128)} %param.19) | copy-start | bytes 294916
  131.6 14.4 %copy-start.7 = (s32[1,1,32,64]{3,2,1,0:T(8,128)S(1)}, s32[1,1,32,64]{3,2,1,0:T(8,128)}, u32[]{:S(2)}) copy-start(s32[1,1,32,64]{3,2,1,0:T(8,128)} %param.22) | copy-start | bytes 24580
  131.6 14.5 %copy-start.4 = (s32[1,1,32,64]{3,2,1,0:T(8,128)S(1)}, s32[1,1,32,64]{3,2,1,0:T(8,128)}, u32[]{:S(2)}) copy-start(s32[1,1,32,64]{3,2,1,0:T(8,128)} %param.21) | copy-start | bytes 24580
  131.6 14.6 %copy-start.5 = (s32[8]{0:T(128)S(1)}, s32[8]{0:T(128)}, u32[]{:S(2)}) copy-start(s32[8]{0:T(128)} %param.24) | copy-start | bytes 100
  131.6 15.3 %copy-start.6 = (f32[8]{0:T(128)S(1)}, f32[8]{0:T(128)}, u32[]{:S(2)}) copy-start(f32[8]{0:T(128)} %param.25) | copy-start | bytes 100
  132.5 27.2 %all-to-all-start = ((f32[32,16,256]{2,1,0:T(8,128)}), f32[32,16,256]{2,1,0:T(8,128)S(1)}, u32[]{:S(2)}, u32[]{:S(2)}) async-start(f32[32,16,256]{2,1,0:T(8,128)} %stack.2), calls=%async_computation | async-start | bytes 1048576 | tf_op jit(solution)/shard_map/all_to_all | solution.py:66
  254.0 1.7 copy-start.8
  255.8 40.1 %copy-start.2 = (f32[1,1,128,128]{3,2,1,0:T(8,128)S(1)}, f32[1,1,128,128]{3,2,1,0:T(8,128)}, u32[]{:S(2)}) copy-start(f32[1,1,128,128]{3,2,1,0:T(8,128)} %param.23) | copy-start | bytes 196612
  265.1 16.7 %all-to-all-start.1 = ((f32[32,1,64]{2,1,0:T(1,128)}), f32[32,1,64]{2,1,0:T(1,128)S(1)}, u32[]{:S(2)}, u32[]{:S(2)}) async-start(f32[32,1,64]{2,1,0:T(1,128)} %and_select_fusion), calls=%async_computation.1 | async-start | bytes 32768 | tf_op jit(solution)/shard_map/all_to_all | solution.py:76
  295.8 16.6 %collective-permute-start.2 = (f32[3,128]{1,0:T(4,128)S(1)}, f32[3,128]{1,0:T(4,128)S(1)}, u32[]{:S(2)}, u32[]{:S(2)}) collective-permute-start(f32[3,128]{1,0:T(4,128)S(1)} %get-tuple-element.41), channel_id=1, source_target_pairs={{1,0},{2,1},{3,2},{4,3},{5,4},{6,5},{7,6},{8,7},{9,8},{10,9},{11,1... | collective-permute-start | bytes 4616 | tf_op jit(solution)/shard_map/ppermute | solution.py:29
  298.8 13.7 %collective-permute-start.1 = (f32[3,128]{1,0:T(4,128)S(1)}, f32[3,128]{1,0:T(4,128)S(1)}, u32[]{:S(2)}, u32[]{:S(2)}) collective-permute-start(f32[3,128]{1,0:T(4,128)S(1)} %get-tuple-element.40), channel_id=1, source_target_pairs={{0,1},{1,2},{2,3},{3,4},{4,5},{5,6},{6,7},{7,8},{8,9},{9,10},{10,1... | collective-permute-start | bytes 4616 | tf_op jit(solution)/shard_map/ppermute | solution.py:27
